TPU v7x, 32 devices: a whole 2x2x4 slice. The times are simulated.
32 devices in a mesh: groups: 2 (over y), ctx: 4 (over z), head: 2 (over x), rep: 2 (over core).
Axes of the slice: x: 2, y: 2, z: 4, core: 2. Of those that a mesh axis runs over, the one named last changes fastest.
Arguments:
- queries: bfloat16 [4, 512, 1024], P(('groups', 'rep'), 'ctx', 'head'), parts along dimension 0, may hold values from -6 to 6
- per_head_keys: bfloat16 [4, 512, 1024], P(('groups', 'rep'), 'ctx', 'head'), parts along dimension 0, may hold values from -6 to 6
- value_rows: bfloat16 [4, 512, 1024], P(('groups', 'rep'), 'ctx', 'head'), parts along dimension 0, may hold values from -6 to 6
- gate_logits: bfloat16 [4, 512, 1024], P(('groups', 'rep'), 'ctx', 'head'), parts along dimension 0, may hold values from -16 to 4
- gate_bias: float32 [1024], P('head'), may hold values from -1 to 13
- value_weight: float32 [1024], P('head'), may hold values from -0.1875 to 0.1875
- targets: float32 [4, 512], P(('groups', 'rep'), 'ctx'), parts along dimension 0, may hold values from -6 to 6
- mask_ids: int32 [4, 4], P(('groups', 'rep'), 'ctx'), parts along dimension 0, may hold values from 0 to 3
- segment_starts: int32 [4, 512], P(('groups', 'rep'), 'ctx'), parts along dimension 0, may hold values 0 or 1
Outputs:
- value_pred: float32 [4, 512], P(('groups', 'rep'), 'ctx'), parts along dimension 0
- query_gradient_rows: bfloat16 [4, 512, 1024], P(('groups', 'rep'), 'ctx', 'head'), parts along dimension 0
- grad_keys: bfloat16 [4, 512, 1024], P(('groups', 'rep'), 'ctx', 'head'), parts along dimension 0
- grad_values: bfloat16 [4, 512, 1024], P(('groups', 'rep'), 'ctx', 'head'), parts along dimension 0
- grad_gate_logits: bfloat16 [4, 512, 1024], P(('groups', 'rep'), 'ctx', 'head'), parts along dimension 0
- grad_gate_bias: float32 [2048], P(('groups', 'head')), parts along dimension 0
- grad_value_weight: float32 [2048], P(('groups', 'head')), parts along dimension 0
There are 2 independent parts, one for each index of `groups`. A program takes and returns all parts, laid end to end along the dimension named above; an argument that names none is the same for every part. Nothing has to cross between parts.
Inputs may be any that keep to these rules, and one draw needn't show every extreme that they name: `mask_ids`: the window kind of each block of 128 positions. `segment_starts`: flags of segment starts.
All inputs are finite; a program needn't handle non-finite values. No bound on the sum of `segment_starts` on one device may be relied on, other than what follows from the above.
Results may differ from a plain program's by a relative error of at most 0.013.
Values sent between devices are 32-bit elements; how exact they have to be, the bound alone decides.
No kernel may reach another device: no remote copies, remote signals or barrier semaphores. Data moves between devices by JAX's collectives and lax.ppermute only.
A program may use at most 64 MiB of HBM per device.

v0:
```python
import jax
import jax.numpy as jnp
from jax import lax
from jax.sharding import PartitionSpec as P

DK = 128
DV = 128
epsilon = 1.0
gate_scale = 16.0
highest = lax.Precision.HIGHEST


def from_behind(value, axis, by):
    length = lax.axis_size(axis)
    pairs = [(i, i + by) for i in range(length) if 0 <= i + by < length]
    return lax.ppermute(value, axis, pairs)


def block_pass(query_in, key_in, value_in, decay, start_flags, kind_ids):
    blocks = kind_ids.shape[0]
    block_len = query_in.shape[0] // blocks
    head_count = query_in.shape[1]
    channels = query_in.shape[2]
    value_width = value_in.shape[2]
    query_f = query_in.astype(jnp.float32).reshape(blocks, block_len, head_count, channels)
    key_f = key_in.astype(jnp.float32).reshape(blocks, block_len, head_count, channels)
    value_bf = value_in.reshape(blocks, block_len, head_count, value_width)
    value_f = value_bf.astype(jnp.float32)
    log_cum = jnp.cumsum(decay.reshape(blocks, block_len, head_count, channels), axis=1)
    log_last = log_cum[:, -1]
    segment = jnp.cumsum(start_flags.reshape(blocks, block_len), axis=1, dtype=jnp.int32)
    alive_mask = (segment == 0).astype(jnp.float32)
    offsets = jnp.arange(block_len, dtype=jnp.int32)
    distance = offsets[:, None] - offsets[None, :]
    window = block_len // jnp.left_shift(jnp.ones_like(kind_ids), kind_ids)
    live_pairs = (
        (segment[:, :, None] == segment[:, None, :])
        & (distance[None] >= 0)
        & (distance[None] < window[:, None, None])
    )
    query_dec = query_f * jnp.exp(log_cum) * channels ** (-0.5)
    key_dec = key_f * jnp.exp(-log_cum)
    scores = jnp.einsum("bihc,bjhc->bhij", query_dec, key_dec, precision=highest)
    block_probs = jnp.where(live_pairs[:, None], scores, 0.0).astype(jnp.bfloat16)
    inner_part = jnp.einsum(
        "bhij,bjhd->bihd", block_probs, value_bf, preferred_element_type=jnp.float32
    )
    tail_mask = (segment == segment[:, -1:]).astype(jnp.float32)
    key_tail = key_f * jnp.exp(log_last[:, None] - log_cum) * tail_mask[:, :, None, None]
    block_state = jnp.einsum("bjhc,bjhd->bhcd", key_tail, value_f, precision=highest)
    block_decay = jnp.exp(log_last) * alive_mask[:, -1][:, None, None]

    def advance(carried_in, block_items):
        state_now, factor = carried_in
        new_state = state_now * block_items[1][..., None] + block_items[0]
        return ((new_state, factor * block_items[1]), (state_now, factor))

    initial = (
        jnp.zeros((head_count, channels, value_width), jnp.float32),
        jnp.ones((head_count, channels), jnp.float32),
    )
    finals, befores = lax.scan(advance, initial, (block_state, block_decay))
    query_live = query_dec * alive_mask[:, :, None, None]
    outer_part = jnp.einsum("bihc,bhcd->bihd", query_live, befores[0], precision=highest)
    carried = query_live * befores[1][:, None]
    attended = (inner_part + outer_part).reshape(blocks * block_len, head_count, value_width)
    return (
        attended,
        finals[0],
        finals[1],
        carried.reshape(blocks * block_len, head_count, channels),
    )


def on_device(
    queries,
    per_head_keys,
    value_rows,
    gate_logits,
    gate_bias,
    value_weight,
    targets,
    mask_ids,
    segment_starts,
):
    token_count = queries.shape[1]
    head_count = gate_bias.shape[0] // DK

    def to_heads(array):
        return array[0].reshape(token_count, head_count, -1)

    start_flags = segment_starts[0]
    kind_ids = mask_ids[0]

    def local_terms(query_in, key_in, value_in, logit_in, bias_in):
        decay = jax.nn.log_sigmoid(logit_in.astype(jnp.float32) + bias_in) / gate_scale
        return block_pass(query_in, key_in, value_in, decay, start_flags, kind_ids)

    local_out, pull_local = jax.vjp(
        local_terms,
        to_heads(queries),
        to_heads(per_head_keys),
        to_heads(value_rows),
        to_heads(gate_logits),
        gate_bias.reshape(head_count, DK),
    )
    attended_local, state_local, decay_local, carried = local_out

    def pass_state(position, incoming):
        return from_behind(incoming * decay_local[..., None] + state_local, "ctx", 1)

    state_in = lax.fori_loop(0, lax.axis_size("ctx") - 1, pass_state, jnp.zeros_like(state_local))
    attended = attended_local + jnp.einsum("thc,hcd->thd", carried, state_in, precision=highest)

    def value_head(attended_in, weight_in):
        normed = attended_in * lax.rsqrt(
            jnp.mean(attended_in * attended_in, axis=-1, keepdims=True) + epsilon
        )
        return jnp.einsum("thd,hd->t", normed, weight_in, precision=highest)

    partial_value, pull_value = jax.vjp(value_head, attended, value_weight.reshape(head_count, DV))
    value_pred = lax.psum(partial_value, "head")
    residual = value_pred - targets[0]
    grad_attended, grad_weight = pull_value(residual)
    grad_carried = jnp.einsum("thd,hcd->thc", grad_attended, state_in, precision=highest)
    grad_direct = jnp.einsum("thc,thd->hcd", carried, grad_attended, precision=highest)

    def pass_grad(position, incoming):
        return from_behind(grad_direct + decay_local[..., None] * incoming, "ctx", -1)

    grad_state = lax.fori_loop(0, lax.axis_size("ctx") - 1, pass_grad, jnp.zeros_like(grad_direct))
    grad_decay = jnp.sum(state_in * grad_state, axis=-1)
    grad_query, grad_key, grad_value, grad_logit, grad_bias = pull_local(
        (grad_attended, grad_state, grad_decay, grad_carried)
    )
    token_total = token_count * lax.axis_size("ctx") * lax.axis_size("rep")
    bias_total, weight_total = lax.psum(
        (grad_bias.reshape(-1), grad_weight.reshape(-1)), ("ctx", "rep")
    )
    return (
        value_pred[None],
        grad_query.reshape(1, token_count, -1),
        grad_key.reshape(1, token_count, -1),
        grad_value.reshape(1, token_count, -1),
        grad_logit.reshape(1, token_count, -1),
        bias_total / token_total,
        weight_total / token_total,
    )


def solution(mesh):
    in_specs = (
        P(("groups", "rep"), "ctx", "head"),
        P(("groups", "rep"), "ctx", "head"),
        P(("groups", "rep"), "ctx", "head"),
        P(("groups", "rep"), "ctx", "head"),
        P("head"),
        P("head"),
        P(("groups", "rep"), "ctx"),
        P(("groups", "rep"), "ctx"),
        P(("groups", "rep"), "ctx"),
    )
    out_specs = (
        P(("groups", "rep"), "ctx"),
        P(("groups", "rep"), "ctx", "head"),
        P(("groups", "rep"), "ctx", "head"),
        P(("groups", "rep"), "ctx", "head"),
        P(("groups", "rep"), "ctx", "head"),
        P(("groups", "head")),
        P(("groups", "head")),
    )
    return jax.shard_map(
        on_device, mesh=mesh, in_specs=in_specs, out_specs=out_specs, check_vma=False
    )
```

profile of v0, /device:TPU:0, one launch (start us, length us, event | category | flops | bytes accessed | tf_op | source)
XLA Modules:
  0.0 105.6 jit_solution(13447743507898511805)
XLA Ops:
  0.6 1.0 reshape.486
  1.7 0.4 fusion.9
  2.0 0.6 copy-done.13
  3.0 0.6 slice.11
  4.2 0.6 slice.12
  4.8 1.2 %compare_convert_fusion.1 = (f32[128]{0:T(128)}, f32[128]{0:T(128)S(1)}) fusion(s32[1,128]{1,0:T(1,128)S(1)} %reduce_window_sum.35, s32[]{:T(128)} %bitcast.14), kind=kLoop, calls=%fused_computation.129 | loop fusion | flops 512 | bytes 1540 | tf_op jit(solution)/shard_map/jvp()/convert_element_type | solution.py:32
  6.3 0.8 copy-done.2
  7.1 0.5 convolution_add_fusion
  7.6 28.2 %while.4 = (s32[]{:T(128)}, f32[4,128,128]{2,1,0:T(8,128)S(1)}, f32[4,128]{1,0:T(4,128)S(1)}, f32[4,128,128]{2,1,0:T(8,128)S(1)}, s32[]{:T(128)}) while((s32[]{:T(128)}, f32[4,128,128]{2,1,0:T(8,128)S(1)}, f32[4,128]{1,0:T(4,128)S(1)}, f32[4,128,128]{2,1,0:T(8,128)S(1)}, s32[]{:T(128)}) %tuple.61), condition=%wide.region_3.4_spmd, body=%wide.region_2.3_spmd.sunk | while | flops 131074 | bytes 1837157 | solution.py:112
  7.8 4.9 %collective-permute-start = (f32[4,128,128]{2,1,0:T(8,128)S(1)}, f32[4,128,128]{2,1,0:T(8,128)S(1)}, u32[]{:S(2)}, u32[]{:S(2)}) collective-permute-start(f32[4,128,128]{2,1,0:T(8,128)S(1)} %multiply_add_fusion.5), channel_id=1, source_target_pairs={{0,4},{4,8},{8,12},{1,5},{5,9},{9,13},{2,6},{6,10},{10,14},{3,7},{... | collective-permute-start | bytes 786440 | tf_op jit(solution)/shard_map/while/body/eval_jaxpr/ppermute | solution.py:16
  12.7 5.5 %collective-permute-done = f32[4,128,128]{2,1,0:T(8,128)S(1)} collective-permute-done((f32[4,128,128]{2,1,0:T(8,128)S(1)}, f32[4,128,128]{2,1,0:T(8,128)S(1)}, u32[]{:S(2)}, u32[]{:S(2)}) %collective-permute-start) | collective-permute-done | bytes 262176 | tf_op jit(solution)/shard_map/while/body/eval_jaxpr/ppermute | solution.py:16
  18.4 4.4 %collective-permute-start = (f32[4,128,128]{2,1,0:T(8,128)S(1)}, f32[4,128,128]{2,1,0:T(8,128)S(1)}, u32[]{:S(2)}, u32[]{:S(2)}) collective-permute-start(f32[4,128,128]{2,1,0:T(8,128)S(1)} %multiply_add_fusion.5), channel_id=1, source_target_pairs={{0,4},{4,8},{8,12},{1,5},{5,9},{9,13},{2,6},{6,10},{10,14},{3,7},{... | collective-permute-start | bytes 786440 | tf_op jit(solution)/shard_map/while/body/eval_jaxpr/ppermute | solution.py:16
  22.8 4.7 %collective-permute-done = f32[4,128,128]{2,1,0:T(8,128)S(1)} collective-permute-done((f32[4,128,128]{2,1,0:T(8,128)S(1)}, f32[4,128,128]{2,1,0:T(8,128)S(1)}, u32[]{:S(2)}, u32[]{:S(2)}) %collective-permute-start) | collective-permute-done | bytes 262176 | tf_op jit(solution)/shard_map/while/body/eval_jaxpr/ppermute | solution.py:16
  27.6 4.4 %collective-permute-start = (f32[4,128,128]{2,1,0:T(8,128)S(1)}, f32[4,128,128]{2,1,0:T(8,128)S(1)}, u32[]{:S(2)}, u32[]{:S(2)}) collective-permute-start(f32[4,128,128]{2,1,0:T(8,128)S(1)} %multiply_add_fusion.5), channel_id=1, source_target_pairs={{0,4},{4,8},{8,12},{1,5},{5,9},{9,13},{2,6},{6,10},{10,14},{3,7},{... | collective-permute-start | bytes 786440 | tf_op jit(solution)/shard_map/while/body/eval_jaxpr/ppermute | solution.py:16
  32.0 3.9 %collective-permute-done = f32[4,128,128]{2,1,0:T(8,128)S(1)} collective-permute-done((f32[4,128,128]{2,1,0:T(8,128)S(1)}, f32[4,128,128]{2,1,0:T(8,128)S(1)}, u32[]{:S(2)}, u32[]{:S(2)}) %collective-permute-start) | collective-permute-done | bytes 262176 | tf_op jit(solution)/shard_map/while/body/eval_jaxpr/ppermute | solution.py:16
  37.0 0.7 fusion.2
  37.9 0.7 fusion.1
  38.6 0.7 multiply_reduce_fusion.2
  39.4 0.6 copy-done.4
  40.3 4.9 %psum.21 = f32[128]{0:T(128)S(1)} all-reduce(f32[128]{0:T(128)S(1)} %convolution_bitcast_fusion.2), channel_id=1, replica_groups=mesh['groups'=2,'ctx'=4,'head'=2,'rep'=2] {'head'}, use_global_device_ids=true, to_apply=%region_5.6 | all-reduce | flops 128 | bytes 1024 | tf_op jit(solution)/shard_map/psum | solution.py:122
  45.2 0.5 copy-done.15
  45.9 0.7 fusion.60
  46.6 28.3 %while.5 = (s32[]{:T(128)}, f32[4,128,128]{2,1,0:T(8,128)S(1)}, f32[4,128]{1,0:T(4,128)S(1)}, f32[4,128,128]{2,1,0:T(8,128)S(1)}, s32[]{:T(128)}) while((s32[]{:T(128)}, f32[4,128,128]{2,1,0:T(8,128)S(1)}, f32[4,128]{1,0:T(4,128)S(1)}, f32[4,128,128]{2,1,0:T(8,128)S(1)}, s32[]{:T(128)}) %tuple.67), condition=%wide.region_8.9_spmd, body=%wide.region_7.8_spmd.sunk | while | flops 131074 | bytes 1837157 | solution.py:131
  46.8 1.3 %collective-permute-start.1 = (f32[4,128,128]{2,1,0:T(8,128)S(1)}, f32[4,128,128]{2,1,0:T(8,128)S(1)}, u32[]{:S(2)}, u32[]{:S(2)}) collective-permute-start(f32[4,128,128]{2,1,0:T(8,128)S(1)} %multiply_add_fusion.6), channel_id=1, source_target_pairs={{4,0},{8,4},{12,8},{5,1},{9,5},{13,9},{6,2},{10,6},{14,10},{7,3},{... | collective-permute-start | bytes 786440 | tf_op jit(solution)/shard_map/while/body/eval_jaxpr/ppermute | solution.py:16
  48.1 7.9 %collective-permute-done.1 = f32[4,128,128]{2,1,0:T(8,128)S(1)} collective-permute-done((f32[4,128,128]{2,1,0:T(8,128)S(1)}, f32[4,128,128]{2,1,0:T(8,128)S(1)}, u32[]{:S(2)}, u32[]{:S(2)}) %collective-permute-start.1) | collective-permute-done | bytes 262176 | tf_op jit(solution)/shard_map/while/body/eval_jaxpr/ppermute | solution.py:16
  56.1 1.3 %collective-permute-start.1 = (f32[4,128,128]{2,1,0:T(8,128)S(1)}, f32[4,128,128]{2,1,0:T(8,128)S(1)}, u32[]{:S(2)}, u32[]{:S(2)}) collective-permute-start(f32[4,128,128]{2,1,0:T(8,128)S(1)} %multiply_add_fusion.6), channel_id=1, source_target_pairs={{4,0},{8,4},{12,8},{5,1},{9,5},{13,9},{6,2},{10,6},{14,10},{7,3},{... | collective-permute-start | bytes 786440 | tf_op jit(solution)/shard_map/while/body/eval_jaxpr/ppermute | solution.py:16
  57.4 8.8 %collective-permute-done.1 = f32[4,128,128]{2,1,0:T(8,128)S(1)} collective-permute-done((f32[4,128,128]{2,1,0:T(8,128)S(1)}, f32[4,128,128]{2,1,0:T(8,128)S(1)}, u32[]{:S(2)}, u32[]{:S(2)}) %collective-permute-start.1) | collective-permute-done | bytes 262176 | tf_op jit(solution)/shard_map/while/body/eval_jaxpr/ppermute | solution.py:16
  66.3 1.3 %collective-permute-start.1 = (f32[4,128,128]{2,1,0:T(8,128)S(1)}, f32[4,128,128]{2,1,0:T(8,128)S(1)}, u32[]{:S(2)}, u32[]{:S(2)}) collective-permute-start(f32[4,128,128]{2,1,0:T(8,128)S(1)} %multiply_add_fusion.6), channel_id=1, source_target_pairs={{4,0},{8,4},{12,8},{5,1},{9,5},{13,9},{6,2},{10,6},{14,10},{7,3},{... | collective-permute-start | bytes 786440 | tf_op jit(solution)/shard_map/while/body/eval_jaxpr/ppermute | solution.py:16
  67.6 7.3 %collective-permute-done.1 = f32[4,128,128]{2,1,0:T(8,128)S(1)} collective-permute-done((f32[4,128,128]{2,1,0:T(8,128)S(1)}, f32[4,128,128]{2,1,0:T(8,128)S(1)}, u32[]{:S(2)}, u32[]{:S(2)}) %collective-permute-start.1) | collective-permute-done | bytes 262176 | tf_op jit(solution)/shard_map/while/body/eval_jaxpr/ppermute | solution.py:16
  74.9 0.8 multiply_reduce_fusion
  75.7 0.5 fusion.100
  76.3 0.5 fusion.33
  77.3 0.6 fusion.79
  77.9 0.8 copy.145
  78.8 0.6 fusion.56
  79.5 0.4 fusion.75
  80.2 1.4 %fusion.98 = (f32[4,128]{1,0:T(4,128)S(1)}, bf16[1,128,4,128]{3,2,1,0:T(4,128)(2,1)S(1)}, bf16[1,128,4,128]{3,2,1,0:T(4,128)(2,1)S(1)}, f32[1,128,4,128]{3,2,1,0:T(4,128)S(1)}) fusion(f32[1,128,4,128]{3,2,1,0:T(4,128)S(1)} %fusion.9, f32[4,128]{1,0:T(4,128)S(1)} %slice_bitcast_fusion, f32[1,128,4,128]{3,2,1,0:T(4,128)S(1)} %copy.167, f32[128]{0:T(128)} %copy-done.9, ...), kind=kLoop, calls=%fused_computation.145 | loop fusion | flops 1048064 | bytes 2364416 | tf_op jit(solution)/shard_map/transpose(jvp())/reduce_sum | solution.py:49
  81.8 0.7 copy-done
  82.6 0.8 reshape.491
  83.4 2.9 %fusion.55 = (f32[4,128]{1,0:T(4,128)S(1)}, f32[1,128,4,128]{3,2,1,0:T(4,128)S(1)}) fusion(f32[128,4,128]{2,1,0:T(4,128)} %reshape.491, f32[4,128]{1,0:T(4,128)S(1)} %bitcast.191, f32[1,128,4,128]{3,2,1,0:T(4,128)S(1)} %copy.167, f32[4,128,128]{2,0,1:T(4,128)S(1)} %copy.151, f32[1,1,4,128]{3,2,1,0:T(4,128)S(1)} %bitcast_add_fusion.2, ...), kind=kOutput, calls=%fused_computation.89 | output fusion | flops 10354176 | bytes 2105856 | tf_op jit(solution)/shard_map/transpose(jvp(jit(cumsum)))/reduce_window_sum | solution.py:29
  86.3 0.6 copy-done.6
  87.3 13.6 %all-reduce.1 = (f32[512]{0:T(512)S(1)}, f32[512]{0:T(512)S(1)}) all-reduce(f32[512]{0:T(512)S(1)} %negate_bitcast_fusion, f32[512]{0:T(512)S(1)} %bitcast.192), channel_id=1, replica_groups=mesh['groups'=2,'ctx'=4,'head'=2,'rep'=2] {'ctx','rep'}, use_global_device_ids=true, to_apply=%region_14.15 | all-reduce | flops 1024 | bytes 8192 | tf_op jit(solution)/shard_map/psum | solution.py:137
  100.9 0.6 broadcast_multiply_fusion.1
  101.6 0.9 fusion.15
  102.5 0.6 convolution_convert_fusion
  103.4 0.8 copy.155
  104.1 0.7 convert_element_type.156
  104.9 0.7 convert_element_type.158
  (67 shorter events, 4.5 us)
Async XLA Ops:
  0.6 1.0 copy-start.7
  1.6 4.3 %copy-start.1 = (bf16[1,128,512]{2,1,0:T(8,128)(2,1)S(1)}, bf16[1,128,512]{2,1,0:T(8,128)(2,1)}, u32[]{:S(2)}) copy-start(bf16[1,128,512]{2,1,0:T(8,128)(2,1)} %param.14) | copy-start | bytes 393220
  2.0 0.7 copy-start.13
  6.0 1.1 %copy-start.9 = (f32[128]{0:T(128)}, f32[128]{0:T(128)S(1)}, u32[]{:S(2)}) copy-start(f32[128]{0:T(128)S(1)} %get-tuple-element.174) | copy-start | bytes 1540
  6.1 0.9 copy-start.2
  7.6 29.0 %copy-start.3 = (bf16[1,128,512]{2,1,0:T(8,128)(2,1)S(1)}, bf16[1,128,512]{2,1,0:T(8,128)(2,1)}, u32[]{:S(2)}) copy-start(bf16[1,128,512]{2,1,0:T(8,128)(2,1)} %param.13) | copy-start | bytes 393220
  7.8 10.5 %collective-permute-start = (f32[4,128,128]{2,1,0:T(8,128)S(1)}, f32[4,128,128]{2,1,0:T(8,128)S(1)}, u32[]{:S(2)}, u32[]{:S(2)}) collective-permute-start(f32[4,128,128]{2,1,0:T(8,128)S(1)} %multiply_add_fusion.5), channel_id=1, source_target_pairs={{0,4},{4,8},{8,12},{1,5},{5,9},{9,13},{2,6},{6,10},{10,14},{3,7},{... | collective-permute-start | bytes 786440 | tf_op jit(solution)/shard_map/while/body/eval_jaxpr/ppermute | solution.py:16
  18.4 9.1 %collective-permute-start = (f32[4,128,128]{2,1,0:T(8,128)S(1)}, f32[4,128,128]{2,1,0:T(8,128)S(1)}, u32[]{:S(2)}, u32[]{:S(2)}) collective-permute-start(f32[4,128,128]{2,1,0:T(8,128)S(1)} %multiply_add_fusion.5), channel_id=1, source_target_pairs={{0,4},{4,8},{8,12},{1,5},{5,9},{9,13},{2,6},{6,10},{10,14},{3,7},{... | collective-permute-start | bytes 786440 | tf_op jit(solution)/shard_map/while/body/eval_jaxpr/ppermute | solution.py:16
  27.6 8.3 %collective-permute-start = (f32[4,128,128]{2,1,0:T(8,128)S(1)}, f32[4,128,128]{2,1,0:T(8,128)S(1)}, u32[]{:S(2)}, u32[]{:S(2)}) collective-permute-start(f32[4,128,128]{2,1,0:T(8,128)S(1)} %multiply_add_fusion.5), channel_id=1, source_target_pairs={{0,4},{4,8},{8,12},{1,5},{5,9},{9,13},{2,6},{6,10},{10,14},{3,7},{... | collective-permute-start | bytes 786440 | tf_op jit(solution)/shard_map/while/body/eval_jaxpr/ppermute | solution.py:16
  39.3 0.7 copy-start.4
  40.2 5.0 %copy-start.14 = (f32[1,128]{1,0:T(1,128)S(1)}, f32[1,128]{1,0:T(1,128)}, u32[]{:S(2)}) copy-start(f32[1,128]{1,0:T(1,128)} %param.19) | copy-start | bytes 1540
  45.2 0.5 copy-start.15
  45.7 31.3 %copy-start.5 = (f32[128]{0:T(128)}, f32[128]{0:T(128)S(1)}, u32[]{:S(2)}) copy-start(f32[128]{0:T(128)S(1)} %bitcast_subtract_fusion.1) | copy-start | bytes 1540
  46.8 9.2 %collective-permute-start.1 = (f32[4,128,128]{2,1,0:T(8,128)S(1)}, f32[4,128,128]{2,1,0:T(8,128)S(1)}, u32[]{:S(2)}, u32[]{:S(2)}) collective-permute-start(f32[4,128,128]{2,1,0:T(8,128)S(1)} %multiply_add_fusion.6), channel_id=1, source_target_pairs={{4,0},{8,4},{12,8},{5,1},{9,5},{13,9},{6,2},{10,6},{14,10},{7,3},{... | collective-permute-start | bytes 786440 | tf_op jit(solution)/shard_map/while/body/eval_jaxpr/ppermute | solution.py:16
  56.1 10.1 %collective-permute-start.1 = (f32[4,128,128]{2,1,0:T(8,128)S(1)}, f32[4,128,128]{2,1,0:T(8,128)S(1)}, u32[]{:S(2)}, u32[]{:S(2)}) collective-permute-start(f32[4,128,128]{2,1,0:T(8,128)S(1)} %multiply_add_fusion.6), channel_id=1, source_target_pairs={{4,0},{8,4},{12,8},{5,1},{9,5},{13,9},{6,2},{10,6},{14,10},{7,3},{... | collective-permute-start | bytes 786440 | tf_op jit(solution)/shard_map/while/body/eval_jaxpr/ppermute | solution.py:16
  66.3 8.6 %collective-permute-start.1 = (f32[4,128,128]{2,1,0:T(8,128)S(1)}, f32[4,128,128]{2,1,0:T(8,128)S(1)}, u32[]{:S(2)}, u32[]{:S(2)}) collective-permute-start(f32[4,128,128]{2,1,0:T(8,128)S(1)} %multiply_add_fusion.6), channel_id=1, source_target_pairs={{4,0},{8,4},{12,8},{5,1},{9,5},{13,9},{6,2},{10,6},{14,10},{7,3},{... | collective-permute-start | bytes 786440 | tf_op jit(solution)/shard_map/while/body/eval_jaxpr/ppermute | solution.py:16
  80.2 1.4 %copy-start.11 = (f32[4,128]{1,0:T(4,128)S(1)}, f32[4,128]{1,0:T(4,128)}, u32[]{:S(2)}) copy-start(f32[4,128]{1,0:T(4,128)} %get-tuple-element.145) | copy-start | bytes 6148
  80.2 1.4 %copy-start.12 = (f32[4,128]{1,0:T(4,128)S(1)}, f32[4,128]{1,0:T(4,128)}, u32[]{:S(2)}) copy-start(f32[4,128]{1,0:T(4,128)} %get-tuple-element.146) | copy-start | bytes 6148
  81.7 0.9 copy-start
  82.6 0.8 copy-start.8
  82.6 0.8 copy-start.10
  86.3 0.7 copy-start.6
where the time goes:
time: 106 us
  waiting for transfers between devices  38 us (36%)
  blocking collectives  18.5 us (17%)
  starting transfers between devices  17.6 us (17%)
  local copies, waits for them, and re-layouts  11.5 us (11%)
  other arithmetic  9.63 us (9%)
  matrix products  7.78 us (7%)
  between operations  2.37 us (2%)
    ppermute x6, waiting for transfers between devices, from_behind(): return lax.ppermute(value, axis, pairs)  38 us
    ppermute x6, starting transfers between devices, from_behind(): return lax.ppermute(value, axis, pairs)  17.6 us
    psum x1, blocking collectives, on_device(): lax.psum((grad_bias.reshape(-1), grad_weight.reshape(-1)), ('ctx', 'rep'))  13.6 us
    unnamed x35, local copies, waits for them, and re-layouts  5.02 us
    psum x1, blocking collectives, on_device(): value_pred = lax.psum(partial_value, 'head')  4.94 us
    another operation x2, other arithmetic, block_pass(): jnp.cumsum(decay.reshape(blocks, block_len, head_count, channels), axis=1)  3.28 us
  transfers between devices with their start and end apart: 6, of which 6 were waited for; matrix products, arithmetic and copies ran while one was open for 0% of the time, Pallas kernels for 0%

commit v1 on v0

--- a/solution.py
+++ b/solution.py
@@ -1,3 +1,4 @@
+import functools
 import jax
 import jax.numpy as jnp
 from jax import lax
@@ -8,6 +9,13 @@
 epsilon = 1.0
 gate_scale = 16.0
 highest = lax.Precision.HIGHEST
+
+
+def trace_the_frame(x_part, lane_axis):
+    return jnp.sum(lax.all_gather(x_part, lane_axis), 0)
+
+
+pass_tiles = functools.partial(trace_the_frame, lane_axis="head")
 
 
 def from_behind(value, axis, by):
@@ -119,7 +127,7 @@
         return jnp.einsum("thd,hd->t", normed, weight_in, precision=highest)
 
     partial_value, pull_value = jax.vjp(value_head, attended, value_weight.reshape(head_count, DV))
-    value_pred = lax.psum(partial_value, "head")
+    value_pred = pass_tiles(partial_value)
     residual = value_pred - targets[0]
     grad_attended, grad_weight = pull_value(residual)
     grad_carried = jnp.einsum("thd,hcd->thc", grad_attended, state_in, precision=highest)

time: 106 us -> 106 us (level)
    psum x1 -> x0, blocking collectives: 4.94 us -> none  [on_device(): value_pred = lax.psum(partial_value, 'head')]
    all_gather x0 -> x1, blocking collectives: none -> 4.22 us  [trace_the_frame(): return jnp.sum(lax.all_gather(x_part, lane_axis), 0)]
    unnamed x35 -> x39, local copies, waits for them, and re-layouts: 5.02 us -> 5.68 us
where the time goes in v1:
time: 106 us
  waiting for transfers between devices  38 us (36%)
  blocking collectives  17.8 us (17%)
  starting transfers between devices  17.6 us (17%)
  local copies, waits for them, and re-layouts  12.2 us (12%)
  other arithmetic  9.65 us (9%)
  matrix products  7.77 us (7%)
  between operations  2.37 us (2%)
    ppermute x6, waiting for transfers between devices, from_behind(): return lax.ppermute(value, axis, pairs)  38 us
    ppermute x6, starting transfers between devices, from_behind(): return lax.ppermute(value, axis, pairs)  17.6 us
    psum x1, blocking collectives, on_device(): lax.psum((grad_bias.reshape(-1), grad_weight.reshape(-1)), ('ctx', 'rep'))  13.6 us
    unnamed x39, local copies, waits for them, and re-layouts  5.68 us
    all_gather x1, blocking collectives, trace_the_frame(): return jnp.sum(lax.all_gather(x_part, lane_axis), 0)  4.22 us
    another operation x2, other arithmetic, block_pass(): jnp.cumsum(decay.reshape(blocks, block_len, head_count, channels), axis=1)  3.28 us
  transfers between devices with their start and end apart: 6, of which 6 were waited for; matrix products, arithmetic and copies ran while one was open for 0% of the time, Pallas kernels for 0%

profile of v1, /device:TPU:0, one launch (start us, length us, event | category | flops | bytes accessed | tf_op | source)
XLA Modules:
  0.0 105.5 jit_solution(18294157755191564867)
XLA Ops:
  0.6 1.0 reshape.488
  2.0 0.6 copy-done.17
  3.0 0.6 slice.11
  4.2 0.6 slice.12
  4.8 1.2 %compare_convert_fusion.1 = (f32[128]{0:T(128)}, f32[128]{0:T(128)S(1)}) fusion(s32[1,128]{1,0:T(1,128)S(1)} %reduce_window_sum.35, s32[]{:T(128)} %bitcast.14), kind=kLoop, calls=%fused_computation.129 | loop fusion | flops 512 | bytes 1540 | tf_op jit(solution)/shard_map/jvp()/convert_element_type | solution.py:40
  6.3 0.8 copy-done.2
  7.1 0.5 convolution_add_fusion
  7.6 28.2 %while.4 = (s32[]{:T(128)}, f32[4,128,128]{2,1,0:T(8,128)S(1)}, f32[4,128]{1,0:T(4,128)S(1)}, f32[4,128,128]{2,1,0:T(8,128)S(1)}, s32[]{:T(128)}) while((s32[]{:T(128)}, f32[4,128,128]{2,1,0:T(8,128)S(1)}, f32[4,128]{1,0:T(4,128)S(1)}, f32[4,128,128]{2,1,0:T(8,128)S(1)}, s32[]{:T(128)}) %tuple.62), condition=%wide.region_3.4_spmd, body=%wide.region_2.3_spmd.sunk | while | flops 131074 | bytes 1837157 | solution.py:120
  7.8 4.9 %collective-permute-start = (f32[4,128,128]{2,1,0:T(8,128)S(1)}, f32[4,128,128]{2,1,0:T(8,128)S(1)}, u32[]{:S(2)}, u32[]{:S(2)}) collective-permute-start(f32[4,128,128]{2,1,0:T(8,128)S(1)} %multiply_add_fusion.5), channel_id=1, source_target_pairs={{0,4},{4,8},{8,12},{1,5},{5,9},{9,13},{2,6},{6,10},{10,14},{3,7},{... | collective-permute-start | bytes 786440 | tf_op jit(solution)/shard_map/while/body/eval_jaxpr/ppermute | solution.py:24
  12.7 5.5 %collective-permute-done = f32[4,128,128]{2,1,0:T(8,128)S(1)} collective-permute-done((f32[4,128,128]{2,1,0:T(8,128)S(1)}, f32[4,128,128]{2,1,0:T(8,128)S(1)}, u32[]{:S(2)}, u32[]{:S(2)}) %collective-permute-start) | collective-permute-done | bytes 262176 | tf_op jit(solution)/shard_map/while/body/eval_jaxpr/ppermute | solution.py:24
  18.4 4.4 %collective-permute-start = (f32[4,128,128]{2,1,0:T(8,128)S(1)}, f32[4,128,128]{2,1,0:T(8,128)S(1)}, u32[]{:S(2)}, u32[]{:S(2)}) collective-permute-start(f32[4,128,128]{2,1,0:T(8,128)S(1)} %multiply_add_fusion.5), channel_id=1, source_target_pairs={{0,4},{4,8},{8,12},{1,5},{5,9},{9,13},{2,6},{6,10},{10,14},{3,7},{... | collective-permute-start | bytes 786440 | tf_op jit(solution)/shard_map/while/body/eval_jaxpr/ppermute | solution.py:24
  22.8 4.7 %collective-permute-done = f32[4,128,128]{2,1,0:T(8,128)S(1)} collective-permute-done((f32[4,128,128]{2,1,0:T(8,128)S(1)}, f32[4,128,128]{2,1,0:T(8,128)S(1)}, u32[]{:S(2)}, u32[]{:S(2)}) %collective-permute-start) | collective-permute-done | bytes 262176 | tf_op jit(solution)/shard_map/while/body/eval_jaxpr/ppermute | solution.py:24
  27.6 4.4 %collective-permute-start = (f32[4,128,128]{2,1,0:T(8,128)S(1)}, f32[4,128,128]{2,1,0:T(8,128)S(1)}, u32[]{:S(2)}, u32[]{:S(2)}) collective-permute-start(f32[4,128,128]{2,1,0:T(8,128)S(1)} %multiply_add_fusion.5), channel_id=1, source_target_pairs={{0,4},{4,8},{8,12},{1,5},{5,9},{9,13},{2,6},{6,10},{10,14},{3,7},{... | collective-permute-start | bytes 786440 | tf_op jit(solution)/shard_map/while/body/eval_jaxpr/ppermute | solution.py:24
  32.0 3.9 %collective-permute-done = f32[4,128,128]{2,1,0:T(8,128)S(1)} collective-permute-done((f32[4,128,128]{2,1,0:T(8,128)S(1)}, f32[4,128,128]{2,1,0:T(8,128)S(1)}, u32[]{:S(2)}, u32[]{:S(2)}) %collective-permute-start) | collective-permute-done | bytes 262176 | tf_op jit(solution)/shard_map/while/body/eval_jaxpr/ppermute | solution.py:24
  37.0 0.7 fusion.2
  37.9 0.7 fusion.1
  38.6 0.7 multiply_reduce_fusion.2
  39.4 0.6 copy-done.4
  40.2 4.2 %all-gather.1 = f32[2,1,128]{2,1,0:T(1,128)S(1)} all-gather(f32[1,1,128]{2,1,0:T(1,128)S(1)} %convolution_bitcast_fusion.2), channel_id=2, replica_groups=mesh['groups'=2,'ctx'=4,'head'=2,'rep'=2] {'head'}, dimensions={0}, use_global_device_ids=true | all-gather | bytes 1536 | tf_op jit(solution)/shard_map/all_gather | solution.py:15
  44.5 0.6 copy-done.15
  45.1 0.5 copy-done.13
  45.8 0.7 fusion.60
  46.5 28.3 %while.5 = (s32[]{:T(128)}, f32[4,128,128]{2,1,0:T(8,128)S(1)}, f32[4,128]{1,0:T(4,128)S(1)}, f32[4,128,128]{2,1,0:T(8,128)S(1)}, s32[]{:T(128)}) while((s32[]{:T(128)}, f32[4,128,128]{2,1,0:T(8,128)S(1)}, f32[4,128]{1,0:T(4,128)S(1)}, f32[4,128,128]{2,1,0:T(8,128)S(1)}, s32[]{:T(128)}) %tuple.68), condition=%wide.region_8.9_spmd, body=%wide.region_7.8_spmd.sunk | while | flops 131074 | bytes 1837157 | solution.py:139
  46.7 1.3 %collective-permute-start.1 = (f32[4,128,128]{2,1,0:T(8,128)S(1)}, f32[4,128,128]{2,1,0:T(8,128)S(1)}, u32[]{:S(2)}, u32[]{:S(2)}) collective-permute-start(f32[4,128,128]{2,1,0:T(8,128)S(1)} %multiply_add_fusion.6), channel_id=1, source_target_pairs={{4,0},{8,4},{12,8},{5,1},{9,5},{13,9},{6,2},{10,6},{14,10},{7,3},{... | collective-permute-start | bytes 786440 | tf_op jit(solution)/shard_map/while/body/eval_jaxpr/ppermute | solution.py:24
  48.0 7.9 %collective-permute-done.1 = f32[4,128,128]{2,1,0:T(8,128)S(1)} collective-permute-done((f32[4,128,128]{2,1,0:T(8,128)S(1)}, f32[4,128,128]{2,1,0:T(8,128)S(1)}, u32[]{:S(2)}, u32[]{:S(2)}) %collective-permute-start.1) | collective-permute-done | bytes 262176 | tf_op jit(solution)/shard_map/while/body/eval_jaxpr/ppermute | solution.py:24
  56.0 1.3 %collective-permute-start.1 = (f32[4,128,128]{2,1,0:T(8,128)S(1)}, f32[4,128,128]{2,1,0:T(8,128)S(1)}, u32[]{:S(2)}, u32[]{:S(2)}) collective-permute-start(f32[4,128,128]{2,1,0:T(8,128)S(1)} %multiply_add_fusion.6), channel_id=1, source_target_pairs={{4,0},{8,4},{12,8},{5,1},{9,5},{13,9},{6,2},{10,6},{14,10},{7,3},{... | collective-permute-start | bytes 786440 | tf_op jit(solution)/shard_map/while/body/eval_jaxpr/ppermute | solution.py:24
  57.3 8.8 %collective-permute-done.1 = f32[4,128,128]{2,1,0:T(8,128)S(1)} collective-permute-done((f32[4,128,128]{2,1,0:T(8,128)S(1)}, f32[4,128,128]{2,1,0:T(8,128)S(1)}, u32[]{:S(2)}, u32[]{:S(2)}) %collective-permute-start.1) | collective-permute-done | bytes 262176 | tf_op jit(solution)/shard_map/while/body/eval_jaxpr/ppermute | solution.py:24
  66.2 1.3 %collective-permute-start.1 = (f32[4,128,128]{2,1,0:T(8,128)S(1)}, f32[4,128,128]{2,1,0:T(8,128)S(1)}, u32[]{:S(2)}, u32[]{:S(2)}) collective-permute-start(f32[4,128,128]{2,1,0:T(8,128)S(1)} %multiply_add_fusion.6), channel_id=1, source_target_pairs={{4,0},{8,4},{12,8},{5,1},{9,5},{13,9},{6,2},{10,6},{14,10},{7,3},{... | collective-permute-start | bytes 786440 | tf_op jit(solution)/shard_map/while/body/eval_jaxpr/ppermute | solution.py:24
  67.5 7.3 %collective-permute-done.1 = f32[4,128,128]{2,1,0:T(8,128)S(1)} collective-permute-done((f32[4,128,128]{2,1,0:T(8,128)S(1)}, f32[4,128,128]{2,1,0:T(8,128)S(1)}, u32[]{:S(2)}, u32[]{:S(2)}) %collective-permute-start.1) | collective-permute-done | bytes 262176 | tf_op jit(solution)/shard_map/while/body/eval_jaxpr/ppermute | solution.py:24
  74.8 0.8 multiply_reduce_fusion
  75.6 0.5 fusion.101
  76.2 0.5 fusion.33
  77.2 0.6 fusion.79
  77.8 0.8 copy.176
  78.7 0.6 fusion.56
  79.4 0.4 fusion.75
  80.2 1.4 %fusion.99 = (f32[4,128]{1,0:T(4,128)S(1)}, bf16[1,128,4,128]{3,2,1,0:T(4,128)(2,1)S(1)}, bf16[1,128,4,128]{3,2,1,0:T(4,128)(2,1)S(1)}, f32[1,128,4,128]{3,2,1,0:T(4,128)S(1)}) fusion(f32[1,128,4,128]{3,2,1,0:T(4,128)S(1)} %fusion.9, f32[4,128]{1,0:T(4,128)S(1)} %slice_bitcast_fusion, f32[1,128,4,128]{3,2,1,0:T(4,128)S(1)} %copy.198, f32[128]{0:T(128)} %copy-done.9, ...), kind=kLoop, calls=%fused_computation.146 | loop fusion | flops 1048064 | bytes 2364416 | tf_op jit(solution)/shard_map/transpose(jvp())/reduce_sum | solution.py:57
  81.8 0.7 copy-done
  82.5 0.8 reshape.493
  83.3 2.9 %fusion.55 = (f32[4,128]{1,0:T(4,128)S(1)}, f32[1,128,4,128]{3,2,1,0:T(4,128)S(1)}) fusion(f32[128,4,128]{2,1,0:T(4,128)} %reshape.493, f32[4,128]{1,0:T(4,128)S(1)} %bitcast.196, f32[1,128,4,128]{3,2,1,0:T(4,128)S(1)} %copy.198, f32[4,128,128]{2,0,1:T(4,128)S(1)} %copy.182, f32[1,1,4,128]{3,2,1,0:T(4,128)S(1)} %bitcast_add_fusion.2, ...), kind=kOutput, calls=%fused_computation.89 | output fusion | flops 10354176 | bytes 2105856 | tf_op jit(solution)/shard_map/transpose(jvp(jit(cumsum)))/reduce_window_sum | solution.py:37
  86.2 0.6 copy-done.14
  87.2 13.6 %all-reduce.1 = (f32[512]{0:T(512)S(1)}, f32[512]{0:T(512)S(1)}) all-reduce(f32[512]{0:T(512)S(1)} %negate_bitcast_fusion, f32[512]{0:T(512)S(1)} %bitcast.197), channel_id=1, replica_groups=mesh['groups'=2,'ctx'=4,'head'=2,'rep'=2] {'ctx','rep'}, use_global_device_ids=true, to_apply=%region_14.15 | all-reduce | flops 1024 | bytes 8192 | tf_op jit(solution)/shard_map/psum | solution.py:145
  100.8 0.6 broadcast_multiply_fusion.1
  101.5 0.9 fusion.15
  102.4 0.6 convolution_convert_fusion
  103.3 0.8 copy.186
  104.1 0.7 convert_element_type.156
  104.8 0.7 convert_element_type.158
  (72 shorter events, 4.9 us)
Async XLA Ops:
  0.6 1.0 copy-start.5
  1.6 4.3 %copy-start.1 = (bf16[1,128,512]{2,1,0:T(8,128)(2,1)S(1)}, bf16[1,128,512]{2,1,0:T(8,128)(2,1)}, u32[]{:S(2)}) copy-start(bf16[1,128,512]{2,1,0:T(8,128)(2,1)} %param.14) | copy-start | bytes 393220
  2.0 0.7 copy-start.17
  6.0 1.1 %copy-start.9 = (f32[128]{0:T(128)}, f32[128]{0:T(128)S(1)}, u32[]{:S(2)}) copy-start(f32[128]{0:T(128)S(1)} %get-tuple-element.181) | copy-start | bytes 1540
  6.1 0.9 copy-start.2
  7.6 29.0 %copy-start.3 = (bf16[1,128,512]{2,1,0:T(8,128)(2,1)S(1)}, bf16[1,128,512]{2,1,0:T(8,128)(2,1)}, u32[]{:S(2)}) copy-start(bf16[1,128,512]{2,1,0:T(8,128)(2,1)} %param.13) | copy-start | bytes 393220
  7.8 10.5 %collective-permute-start = (f32[4,128,128]{2,1,0:T(8,128)S(1)}, f32[4,128,128]{2,1,0:T(8,128)S(1)}, u32[]{:S(2)}, u32[]{:S(2)}) collective-permute-start(f32[4,128,128]{2,1,0:T(8,128)S(1)} %multiply_add_fusion.5), channel_id=1, source_target_pairs={{0,4},{4,8},{8,12},{1,5},{5,9},{9,13},{2,6},{6,10},{10,14},{3,7},{... | collective-permute-start | bytes 786440 | tf_op jit(solution)/shard_map/while/body/eval_jaxpr/ppermute | solution.py:24
  18.4 9.1 %collective-permute-start = (f32[4,128,128]{2,1,0:T(8,128)S(1)}, f32[4,128,128]{2,1,0:T(8,128)S(1)}, u32[]{:S(2)}, u32[]{:S(2)}) collective-permute-start(f32[4,128,128]{2,1,0:T(8,128)S(1)} %multiply_add_fusion.5), channel_id=1, source_target_pairs={{0,4},{4,8},{8,12},{1,5},{5,9},{9,13},{2,6},{6,10},{10,14},{3,7},{... | collective-permute-start | bytes 786440 | tf_op jit(solution)/shard_map/while/body/eval_jaxpr/ppermute | solution.py:24
  27.6 8.3 %collective-permute-start = (f32[4,128,128]{2,1,0:T(8,128)S(1)}, f32[4,128,128]{2,1,0:T(8,128)S(1)}, u32[]{:S(2)}, u32[]{:S(2)}) collective-permute-start(f32[4,128,128]{2,1,0:T(8,128)S(1)} %multiply_add_fusion.5), channel_id=1, source_target_pairs={{0,4},{4,8},{8,12},{1,5},{5,9},{9,13},{2,6},{6,10},{10,14},{3,7},{... | collective-permute-start | bytes 786440 | tf_op jit(solution)/shard_map/while/body/eval_jaxpr/ppermute | solution.py:24
  39.3 0.7 copy-start.4
  44.5 0.7 copy-start.15
  45.1 0.5 copy-start.13
  45.6 31.3 %copy-start.7 = (f32[128]{0:T(128)}, f32[128]{0:T(128)S(1)}, u32[]{:S(2)}) copy-start(f32[128]{0:T(128)S(1)} %subtract_bitcast_fusion) | copy-start | bytes 1540
  46.7 9.2 %collective-permute-start.1 = (f32[4,128,128]{2,1,0:T(8,128)S(1)}, f32[4,128,128]{2,1,0:T(8,128)S(1)}, u32[]{:S(2)}, u32[]{:S(2)}) collective-permute-start(f32[4,128,128]{2,1,0:T(8,128)S(1)} %multiply_add_fusion.6), channel_id=1, source_target_pairs={{4,0},{8,4},{12,8},{5,1},{9,5},{13,9},{6,2},{10,6},{14,10},{7,3},{... | collective-permute-start | bytes 786440 | tf_op jit(solution)/shard_map/while/body/eval_jaxpr/ppermute | solution.py:24
  56.0 10.1 %collective-permute-start.1 = (f32[4,128,128]{2,1,0:T(8,128)S(1)}, f32[4,128,128]{2,1,0:T(8,128)S(1)}, u32[]{:S(2)}, u32[]{:S(2)}) collective-permute-start(f32[4,128,128]{2,1,0:T(8,128)S(1)} %multiply_add_fusion.6), channel_id=1, source_target_pairs={{4,0},{8,4},{12,8},{5,1},{9,5},{13,9},{6,2},{10,6},{14,10},{7,3},{... | collective-permute-start | bytes 786440 | tf_op jit(solution)/shard_map/while/body/eval_jaxpr/ppermute | solution.py:24
  66.2 8.6 %collective-permute-start.1 = (f32[4,128,128]{2,1,0:T(8,128)S(1)}, f32[4,128,128]{2,1,0:T(8,128)S(1)}, u32[]{:S(2)}, u32[]{:S(2)}) collective-permute-start(f32[4,128,128]{2,1,0:T(8,128)S(1)} %multiply_add_fusion.6), channel_id=1, source_target_pairs={{4,0},{8,4},{12,8},{5,1},{9,5},{13,9},{6,2},{10,6},{14,10},{7,3},{... | collective-permute-start | bytes 786440 | tf_op jit(solution)/shard_map/while/body/eval_jaxpr/ppermute | solution.py:24
  80.1 1.4 %copy-start.11 = (f32[4,128]{1,0:T(4,128)S(1)}, f32[4,128]{1,0:T(4,128)}, u32[]{:S(2)}) copy-start(f32[4,128]{1,0:T(4,128)} %get-tuple-element.152) | copy-start | bytes 6148
  80.1 1.4 %copy-start.12 = (f32[4,128]{1,0:T(4,128)S(1)}, f32[4,128]{1,0:T(4,128)}, u32[]{:S(2)}) copy-start(f32[4,128]{1,0:T(4,128)} %get-tuple-element.153) | copy-start | bytes 6148
  81.6 0.9 copy-start
  82.5 0.8 copy-start.6
  82.5 0.8 copy-start.10
  86.2 0.7 copy-start.14
  86.2 0.7 copy-start.16
  102.4 0.7 copy-start.8
